TPU v7x, 512 devices: a whole 4x8x8 slice. The times are simulated.
512 devices in a mesh: req: 128 (over y, z, core), tp: 4 (over x).
Axes of the slice: x: 4, y: 8, z: 8, core: 2. Of those that a mesh axis runs over, the one named last changes fastest.
Arguments:
- tokens: bfloat16 [65536, 1024], P('req', 'tp')
- placement: int32 [16384], P('req'), may hold values from 0 to 16383, as said below
- cache_len: int32 [256], P('req'), may hold values from 0 to 1024, as said below
- w_query: bfloat16 [1024, 1024], P(None, 'tp'), may hold values from -0.1875 to 0.1875
- w_key: bfloat16 [1024, 1024], P(None, 'tp'), may hold values from -0.1875 to 0.1875
- w_value: bfloat16 [1024, 1024], P(None, 'tp'), may hold values from -0.1875 to 0.1875
- w_out: bfloat16 [1024, 1024], P('tp'), may hold values from -0.1875 to 0.1875
- k_cache: bfloat16 [256, 1024, 1024], P('req', None, 'tp'), may hold values from -6 to 6
- v_cache: bfloat16 [256, 1024, 1024], P('req', None, 'tp'), may hold values from -6 to 6
- ln_gain: float32 [1024], replicated, may hold values from 0.1 to 1.9
- ln_bias: float32 [1024], replicated, may hold values from -0.5 to 0.5
Outputs:
- mixed: bfloat16 [65536, 1024], P('req', 'tp')
Inputs may be any that keep to these rules, and one draw needn't show every extreme that they name: `placement`: A permutation of the blocks. Of the 128 blocks that arrive on index s of req, exactly one goes to the owner range of every index t of req, and it lands at owner position t * 128 + s. `cache_len`: some request has exactly 1024 cached positions.
All inputs are finite; a program needn't handle non-finite values.
Results may differ from a plain program's by a relative error of at most 0.014.
The roundings to bfloat16 on the way count: a program that leaves them out, or rounds other values in their place, can miss the bound.
Values may be sent and summed in bfloat16 or wider, within the bound.
No kernel may reach another device: no remote copies, remote signals or barrier semaphores. Data moves between devices by JAX's collectives and lax.ppermute only.
A program may use at most 64 MiB of HBM per device.

v0:
```python
import jax
import jax.numpy as jnp
from jax import lax
from jax.sharding import PartitionSpec as P

D = 1024
HEADS = 16


def head_view(array, head_size):
    return array.reshape(array.shape[0], array.shape[1] // head_size, head_size)


def attend_padded(queries, new_keys, new_values, cache_keys, cache_values, length):
    head_size = D // HEADS
    new_count = queries.shape[0]
    span = cache_keys.shape[0]
    keys_all = head_view(jnp.concatenate([cache_keys, new_keys], 0), head_size)
    values_all = head_view(jnp.concatenate([cache_values, new_values], 0), head_size)
    query_heads = head_view(queries, head_size)
    scores = jnp.einsum(
        "qhd,khd->hqk", query_heads, keys_all, preferred_element_type=jnp.float32
    ) * head_size ** (-0.5)
    key_pos = jnp.arange(span + new_count, dtype=jnp.int32)[None, :]
    query_pos = jnp.arange(new_count, dtype=jnp.int32)[:, None]
    valid = jnp.where(key_pos < span, key_pos < length, key_pos - span <= query_pos)
    scores = jnp.where(valid[None], scores, -jnp.inf)
    top = jnp.max(scores, axis=-1, keepdims=True)
    weight = jnp.where(valid[None], jnp.exp(scores - top), 0.0)
    total = jnp.sum(weight, axis=-1)
    context = jnp.einsum(
        "hqk,khd->qhd", weight.astype(jnp.bfloat16), values_all, preferred_element_type=jnp.float32
    )
    context = context / jnp.transpose(total)[:, :, None]
    return context.reshape(new_count, queries.shape[1]).astype(jnp.bfloat16)


def attend_all(queries, new_keys, new_values, k_cache, v_cache, cache_len):
    request_count = k_cache.shape[0]
    req_shape = (request_count, queries.shape[0] // request_count, queries.shape[1])
    context = lax.map(
        lambda items: attend_padded(*items),
        (
            queries.reshape(req_shape),
            new_keys.reshape(req_shape),
            new_values.reshape(req_shape),
            k_cache,
            v_cache,
            cache_len,
        ),
    )
    return context.reshape(queries.shape)


def project_rows(whole, w_query, w_key, w_value):
    queries = jnp.dot(whole, w_query, preferred_element_type=jnp.float32).astype(jnp.bfloat16)
    new_keys = jnp.dot(whole, w_key, preferred_element_type=jnp.float32).astype(jnp.bfloat16)
    new_values = jnp.dot(whole, w_value, preferred_element_type=jnp.float32).astype(jnp.bfloat16)
    return (queries, new_keys, new_values)


def finish_rows(context, local, w_out, ln_gain, ln_bias):
    row_count, feat_width = local.shape
    partial_sum = jnp.dot(context, w_out, preferred_element_type=jnp.float32)
    attended = lax.psum_scatter(
        partial_sum.astype(jnp.bfloat16), "tp", scatter_dimension=1, tiled=True
    ).astype(jnp.float32)
    summed = local.astype(jnp.float32) + attended
    first_sum, square_sum = lax.psum(
        (jnp.sum(summed, axis=1), jnp.sum(summed * summed, axis=1)), "tp"
    )
    row_mean = first_sum / D
    row_var = square_sum / D - row_mean * row_mean
    offset = lax.axis_index("tp") * feat_width
    gain_part = lax.dynamic_slice_in_dim(ln_gain, offset, feat_width, 0)
    bias_part = lax.dynamic_slice_in_dim(ln_bias, offset, feat_width, 0)
    scaled = (summed - row_mean[:, None]) / jnp.sqrt(row_var[:, None] + 1e-05)
    return (scaled * gain_part + bias_part).astype(jnp.bfloat16)


def shards(
    tokens, placement, cache_len, w_query, w_key, w_value, w_out, k_cache, v_cache, ln_gain, ln_bias
):
    row_count, feat_width = tokens.shape
    block_count = placement.shape[0]
    block_rows = row_count // block_count
    per_peer = block_count // lax.axis_size("req")
    send_slot = placement // block_count * per_peer + placement % per_peer
    send_order = (
        jnp.zeros((block_count,), jnp.int32)
        .at[send_slot]
        .set(jnp.arange(block_count, dtype=jnp.int32))
    )

    def to_blocks(array):
        return array.reshape(block_count, block_rows, array.shape[1])

    arrived = lax.all_to_all(
        to_blocks(tokens)[send_order], "req", split_axis=0, concat_axis=0, tiled=True
    ).reshape(row_count, feat_width)
    whole = lax.all_gather(arrived, "tp", axis=1, tiled=True)
    queries, new_keys, new_values = project_rows(whole, w_query, w_key, w_value)
    context = attend_all(queries, new_keys, new_values, k_cache, v_cache, cache_len)
    normed = finish_rows(context, arrived, w_out, ln_gain, ln_bias)
    returned = lax.all_to_all(to_blocks(normed), "req", split_axis=0, concat_axis=0, tiled=True)
    return returned[send_slot].reshape(row_count, feat_width)


def solution(mesh):
    in_specs = (
        P("req", "tp"),
        P("req"),
        P("req"),
        P(None, "tp"),
        P(None, "tp"),
        P(None, "tp"),
        P("tp", None),
        P("req", None, "tp"),
        P("req", None, "tp"),
        P(),
        P(),
    )
    out_specs = P("req", "tp")
    return jax.shard_map(shards, mesh=mesh, in_specs=in_specs, out_specs=out_specs, check_vma=False)
```

profile of v0, /device:TPU:2, one launch (start us, length us, event | category | flops | bytes accessed | tf_op | source)
XLA Modules:
  0.0 176.9 jit_solution(9790313830979759242)
XLA Ops:
  6.5 0.7 compare_select_fusion.1
  7.3 1.0 scatter_custom_fusion
  8.3 1.0 reshape.143
  9.3 0.8 gather_fusion
  10.1 32.7 %all_to_all.10 = bf16[128,4,256]{2,1,0:T(4,128)(2,1)S(1)} all-to-all(bf16[128,4,256]{2,1,0:T(4,128)(2,1)S(1)} %gather_fusion), channel_id=1, replica_groups=mesh['req'=128,'tp'=4] {'req'}, dimensions={0} | all-to-all | bytes 524288 | tf_op jit(solution)/shard_map/all_to_all | solution.py:98
  42.8 0.8 reshape.144
  43.7 22.3 %all-gather.2.cloned.1.call-done = bf16[512,1024]{1,0:T(8,128)(2,1)} async-done(((bf16[512,256]{1,0:T(8,128)(2,1)}), bf16[512,1024]{1,0:T(8,128)(2,1)}) %all-gather.2.cloned.1.call-update) | async-done | bytes 1048592 | tf_op jit(solution)/shard_map/all_gather | solution.py:101
  66.0 2.5 %convolution_convert_fusion.2 = bf16[512,256]{1,0:T(8,128)(2,1)} fusion(bf16[512,1024]{1,0:T(8,128)(2,1)} %all-gather.2.cloned.1.call-done, bf16[1024,256]{1,0:T(8,128)(2,1)S(1)} %copy-done.8), kind=kOutput, calls=%fused_computation.43 | convolution fusion | flops 268566528 | bytes 1835008 | tf_op jit(solution)/shard_map/dot_general | solution.py:56
  68.4 1.1 convolution_convert_fusion.1
  69.6 1.1 convolution_convert_fusion.3
  70.8 23.4 %while.12 = (s32[]{:T(128)}, bf16[2,256,256]{2,1,0:T(8,128)(2,1)}, bf16[2,1024,256]{2,1,0:T(8,128)(2,1)S(1)}, bf16[2,256,256]{2,1,0:T(8,128)(2,1)}, s32[2]{0:T(1...) while((s32[]{:T(128)}, bf16[2,256,256]{2,1,0:T(8,128)(2,1)}, ...), condition=%wide.region_4.5_spmd, body=%wide.region_1.4_spmd.sunk | while | flops 521149696 | bytes 12803309 | solution.py:41
  70.8 0.6 dynamic_slice.59
  71.5 0.7 iota_compare_fusion.4
  72.1 0.2 fusion.76
  72.4 1.1 constant_dynamic-slice_fusion.9
  73.5 0.2 copy.40
  73.7 1.0 constant_dynamic-slice_fusion.10
  74.7 0.1 copy.38
  74.9 2.3 %fusion.77 = f32[4,256]{1,0:T(4,128)S(1)} fusion(pred[256,1280]{1,0:T(8,128)(4,1)S(1)} %fusion.76, bf16[256,4,64]{0,2,1:T(8,128)(2,1)S(1)} %bitcast.53, bf16[256,4,64]{0,2,1:T(8,128)(2,1)S(1)} %bitcast.55, bf16[1024,4,64]{0,2,1:T(8,128)(2,1)S(1)} %bitcast.50), kind=kOutput, calls=%fused_computation.7.clone.1 | convolution fusion | flops 175637760 | bytes 1118208 | tf_op jit(solution)/shard_map/while/body/eval_jaxpr/sub | solution.py:29
  77.3 0.2 copy.37
  77.5 0.9 constant_dynamic-slice_fusion.8
  78.5 3.1 %fusion.78 = bf16[256,4,64]{0,2,1:T(8,128)(2,1)S(1)} fusion(pred[256,1280]{1,0:T(8,128)(4,1)S(1)} %fusion.76, bf16[256,4,64]{0,2,1:T(8,128)(2,1)S(1)} %bitcast.57, bf16[1024,4,64]{0,2,1:T(8,128)(2,1)S(1)} %bitcast.52, bf16[256,4,64]{0,2,1:T(8,128)(2,1)} %bitcast.54, bf16[256,4,64]{0,2,1:T(8,128)(2,1)} %bitcast.56, ...), kind=kOutput, calls=%fused_computation.16.clone.1 | convolution fusion | flops 344852736 | bytes 1904640 | tf_op jit(solution)/shard_map/while/body/eval_jaxpr/hqk,khd->qhd/dot_general | solution.py:31
  81.7 0.1 copy.41
  81.8 0.7 copy-done.6
  82.5 0.6 dynamic_slice.59
  83.2 0.7 iota_compare_fusion.4
  83.9 0.2 fusion.76
  84.1 1.1 constant_dynamic-slice_fusion.9
  85.2 0.2 copy.40
  85.4 1.0 constant_dynamic-slice_fusion.10
  86.7 2.3 %fusion.77 = f32[4,256]{1,0:T(4,128)S(1)} fusion(pred[256,1280]{1,0:T(8,128)(4,1)S(1)} %fusion.76, bf16[256,4,64]{0,2,1:T(8,128)(2,1)S(1)} %bitcast.53, bf16[256,4,64]{0,2,1:T(8,128)(2,1)S(1)} %bitcast.55, bf16[1024,4,64]{0,2,1:T(8,128)(2,1)S(1)} %bitcast.50), kind=kOutput, calls=%fused_computation.7.clone.1 | convolution fusion | flops 175637760 | bytes 1118208 | tf_op jit(solution)/shard_map/while/body/eval_jaxpr/sub | solution.py:29
  89.0 0.2 copy.37
  89.2 0.9 constant_dynamic-slice_fusion.8
  90.3 3.1 %fusion.78 = bf16[256,4,64]{0,2,1:T(8,128)(2,1)S(1)} fusion(pred[256,1280]{1,0:T(8,128)(4,1)S(1)} %fusion.76, bf16[256,4,64]{0,2,1:T(8,128)(2,1)S(1)} %bitcast.57, bf16[1024,4,64]{0,2,1:T(8,128)(2,1)S(1)} %bitcast.52, bf16[256,4,64]{0,2,1:T(8,128)(2,1)} %bitcast.54, bf16[256,4,64]{0,2,1:T(8,128)(2,1)} %bitcast.56, ...), kind=kOutput, calls=%fused_computation.16.clone.1 | convolution fusion | flops 344852736 | bytes 1904640 | tf_op jit(solution)/shard_map/while/body/eval_jaxpr/hqk,khd->qhd/dot_general | solution.py:31
  93.4 0.1 copy.41
  93.5 0.7 copy-done.6
  94.2 2.4 %convolution_convert_fusion = bf16[512,1024]{1,0:T(8,128)(2,1)} fusion(bf16[512,256]{1,0:T(8,128)(2,1)} %bitcast.62, bf16[256,1024]{1,0:T(8,128)(2,1)S(1)} %copy-done), kind=kOutput, calls=%fused_computation.41 | convolution fusion | flops 268959744 | bytes 1835008 | tf_op jit(solution)/shard_map/dot_general | solution.py:64
  96.7 0.8 dynamic_slice.45
  97.4 0.8 dynamic_slice.46
  98.2 27.0 %reduce-scatter.2.cloned.1.call-done = bf16[512,256]{1,0:T(8,128)(2,1)} async-done(((bf16[512,1024]{1,0:T(8,128)(2,1)}), bf16[512,256]{1,0:T(8,128)(2,1)}) %reduce-scatter.2.cloned.1.call-update) | async-done | bytes 262160 | tf_op jit(solution)/shard_map/reduce_scatter | solution.py:65
  125.2 1.2 fusion.46
  126.4 10.6 %all-reduce = (f32[512]{0:T(512)S(1)}, f32[512]{0:T(512)S(1)}) all-reduce(f32[512]{0:T(512)S(1)} %get-tuple-element.124, f32[512]{0:T(512)S(1)} %get-tuple-element.123), channel_id=1, replica_groups=mesh['req'=128,'tp'=4] {'tp'}, use_global_device_ids=true, to_apply=%region_9.10 | all-reduce | flops 1024 | bytes 8192 | tf_op jit(solution)/shard_map/psum | solution.py:69
  137.0 1.2 add_convert_fusion
  138.2 0.8 reshape.149
  138.9 14.5 %all-to-all-start.1 = ((bf16[128,4,256]{2,1,0:T(4,128)(2,1)}), bf16[128,4,256]{2,1,0:T(4,128)(2,1)S(1)}, u32[]{:S(2)}, u32[]{:S(2)}) async-start(bf16[128,4,256]{2,1,0:T(4,128)(2,1)} %reshape.149), calls=%async_computation.2 | async-start | bytes 524288 | tf_op jit(solution)/shard_map/all_to_all | solution.py:105
  153.4 15.1 %all-to-all-done.1 = bf16[128,4,256]{2,1,0:T(4,128)(2,1)S(1)} async-done(((bf16[128,4,256]{2,1,0:T(4,128)(2,1)}), bf16[128,4,256]{2,1,0:T(4,128)(2,1)S(1)}, u32[]{:S(2)}, u32[]{:S(2)}) %all-to-all-start.1) | async-done | bytes 262176 | tf_op jit(solution)/shard_map/all_to_all | solution.py:105
  168.5 0.8 gather_fusion.1
  169.3 0.8 reshape.150
  (49 shorter events, 0.8 us)
Async XLA Ops:
  6.5 87.7 %copy-start = (bf16[256,1024]{1,0:T(8,128)(2,1)S(1)}, bf16[256,1024]{1,0:T(8,128)(2,1)}, u32[]{:S(2)}) copy-start(bf16[256,1024]{1,0:T(8,128)(2,1)} %param.19) | copy-start | bytes 1572868
  6.5 59.4 %all-gather.2.cloned.1.call-start = ((), (), s32[]{:S(2)}) async-start(), calls=%async_computation.3 | async-start | bytes 1310720 | tf_op jit(solution)/shard_map/all_gather | solution.py:101
  9.3 56.7 %copy-start.8 = (bf16[1024,256]{1,0:T(8,128)(2,1)S(1)}, bf16[1024,256]{1,0:T(8,128)(2,1)}, u32[]{:S(2)}) copy-start(bf16[1024,256]{1,0:T(8,128)(2,1)} %param.16) | copy-start | bytes 1572868
  43.6 24.8 %copy-start.9 = (bf16[1024,256]{1,0:T(8,128)(2,1)S(1)}, bf16[1024,256]{1,0:T(8,128)(2,1)}, u32[]{:S(2)}) copy-start(bf16[1024,256]{1,0:T(8,128)(2,1)} %param.17) | copy-start | bytes 1572868
  43.6 81.6 %reduce-scatter.2.cloned.1.call-start = ((), (), s32[]{:S(2)}) async-start(), calls=%async_computation.4 | async-start | bytes 1310720 | tf_op jit(solution)/shard_map/reduce_scatter | solution.py:65
  65.9 2.5 %copy-start.7 = (bf16[512,1024]{1,0:T(8,128)(2,1)S(1)}, bf16[512,1024]{1,0:T(8,128)(2,1)}, u32[]{:S(2)}) copy-start(bf16[512,1024]{1,0:T(8,128)(2,1)} %all-gather.2.cloned.1.call-done) | copy-start | bytes 3145732
  68.4 1.1 copy-start.10
  69.6 1.2 copy-start.1
  69.6 1.2 copy-start.11
  74.8 2.5 %copy-start.3 = (bf16[1,256,256]{1,2,0:T(8,128)(2,1)}, bf16[1,256,256]{1,2,0:T(8,128)(2,1)S(1)}, u32[]{:S(2)}) copy-start(bf16[1,256,256]{1,2,0:T(8,128)(2,1)S(1)} %copy.38) | copy-start | bytes 393220 | tf_op jit(solution)/shard_map/while
  74.9 2.3 %copy-start.4 = (bf16[1,256,256]{1,2,0:T(8,128)(2,1)}, bf16[1,256,256]{1,2,0:T(8,128)(2,1)S(1)}, u32[]{:S(2)}) copy-start(bf16[1,256,256]{1,2,0:T(8,128)(2,1)S(1)} %copy.39) | copy-start | bytes 393220 | tf_op jit(solution)/shard_map/while
  78.5 3.3 %copy-start.5 = (bf16[2,256,256]{2,1,0:T(8,128)(2,1)S(1)}, bf16[2,256,256]{2,1,0:T(8,128)(2,1)}, u32[]{:S(2)}) copy-start(bf16[2,256,256]{2,1,0:T(8,128)(2,1)} %get-tuple-element.222) | copy-start | bytes 786436 | tf_op jit(solution)/shard_map/while
  81.8 0.7 copy-start.6
  86.5 2.5 %copy-start.3 = (bf16[1,256,256]{1,2,0:T(8,128)(2,1)}, bf16[1,256,256]{1,2,0:T(8,128)(2,1)S(1)}, u32[]{:S(2)}) copy-start(bf16[1,256,256]{1,2,0:T(8,128)(2,1)S(1)} %copy.38) | copy-start | bytes 393220 | tf_op jit(solution)/shard_map/while
  86.6 2.3 %copy-start.4 = (bf16[1,256,256]{1,2,0:T(8,128)(2,1)}, bf16[1,256,256]{1,2,0:T(8,128)(2,1)S(1)}, u32[]{:S(2)}) copy-start(bf16[1,256,256]{1,2,0:T(8,128)(2,1)S(1)} %copy.39) | copy-start | bytes 393220 | tf_op jit(solution)/shard_map/while
  90.2 3.3 %copy-start.5 = (bf16[2,256,256]{2,1,0:T(8,128)(2,1)S(1)}, bf16[2,256,256]{2,1,0:T(8,128)(2,1)}, u32[]{:S(2)}) copy-start(bf16[2,256,256]{2,1,0:T(8,128)(2,1)} %get-tuple-element.222) | copy-start | bytes 786436 | tf_op jit(solution)/shard_map/while
  93.5 0.7 copy-start.6
  94.2 31.0 %copy-start.2 = (bf16[512,256]{1,0:T(8,128)(2,1)S(1)}, bf16[512,256]{1,0:T(8,128)(2,1)}, u32[]{:S(2)}) copy-start(bf16[512,256]{1,0:T(8,128)(2,1)} %reshape.144) | copy-start | bytes 786436
  138.9 29.6 %all-to-all-start.1 = ((bf16[128,4,256]{2,1,0:T(4,128)(2,1)}), bf16[128,4,256]{2,1,0:T(4,128)(2,1)S(1)}, u32[]{:S(2)}, u32[]{:S(2)}) async-start(bf16[128,4,256]{2,1,0:T(4,128)(2,1)} %reshape.149), calls=%async_computation.2 | async-start | bytes 524288 | tf_op jit(solution)/shard_map/all_to_all | solution.py:105
Sparse Core Ops, SparseCore 0:
  43.7 22.1 all-gather.1
  96.8 28.3 reduce-scatter.1
where the time goes:
time: 178 us; the launch traced here: 177 us
  waiting for transfers between devices  64.4 us (36%)
  blocking collectives  43.3 us (24%)
  matrix products  18.1 us (10%)
  local copies, waits for them, and re-layouts  18 us (10%)
  starting transfers between devices  14.5 us (8%)
  between operations  13.5 us (8%)
  other arithmetic  4.9 us (3%)
    all_to_all x1, blocking collectives, shards(): lax.all_to_all(to_blocks(tokens)[send_order], 'req', split_axis=0, concat...  32.7 us
    reduce_scatter x1, waiting for transfers between devices, finish_rows(): lax.psum_scatter(partial_sum.astype(jnp.bfloat16), 'tp', scatter_dimensio...  27 us
    all_gather x1, waiting for transfers between devices, shards(): whole = lax.all_gather(arrived, 'tp', axis=1, tiled=True)  22.3 us
    all_to_all x1, waiting for transfers between devices, shards(): lax.all_to_all(to_blocks(normed), 'req', split_axis=0, concat_axis=0, til...  15.1 us
    all_to_all x1, starting transfers between devices, shards(): lax.all_to_all(to_blocks(normed), 'req', split_axis=0, concat_axis=0, til...  14.5 us
    psum x1, blocking collectives, finish_rows(): lax.psum((jnp.sum(summed, axis=1), jnp.sum(summed * summed, axis=1)), 'tp')  10.6 us
    dynamic_slice x18, local copies, waits for them, and re-layouts, attend_all(): lax.map(lambda items: attend_padded(*items), (queries.reshape(req_shape),...  8.77 us
    dot_general x2, matrix products, attend_padded(): jnp.einsum('hqk,khd->qhd', weight.astype(jnp.bfloat16), values_all, prefe...  6.26 us
  transfers between devices with their start and end apart: 3, of which 3 were waited for; matrix products, arithmetic and copies ran while one was open for 1% of the time, Pallas kernels for 0%

commit v1 on v0

--- a/solution.py
+++ b/solution.py
@@ -5,6 +5,13 @@
 
 D = 1024
 HEADS = 16
+
+
+def wrap_ticks(block_here, axis_no):
+    x_new = list(block_here.shape[1:])
+    x_new[axis_no] *= block_here.shape[0]
+    answer = jnp.moveaxis(block_here, 0, axis_no).reshape(x_new)
+    return answer
 
 
 def head_view(array, head_size):
@@ -98,7 +105,25 @@
     arrived = lax.all_to_all(
         to_blocks(tokens)[send_order], "req", split_axis=0, concat_axis=0, tiled=True
     ).reshape(row_count, feat_width)
-    whole = lax.all_gather(arrived, "tp", axis=1, tiled=True)
+    extent = jax.lax.psum(1, "tp")
+    arrivals = tuple(((rr, (rr + 1) % extent) for rr in range(extent)))
+    kept_rows = tuple(((src_i, pp) for pp, src_i in arrivals))
+    carry_out, state_next = ([], [])
+    s = 0
+    while s < extent - 1:
+        if s % 2 == 0:
+            carry_out.append(
+                jax.lax.ppermute(carry_out[-1] if carry_out else arrived, "tp", arrivals)
+            )
+        else:
+            raw_out = jax.lax.ppermute(state_next[-1] if state_next else arrived, "tp", kept_rows)
+            state_next.append(raw_out)
+        s += 1
+    even = jnp.stack([*carry_out[::-1], arrived, *state_next], 0)
+    r1 = jax.lax.axis_index("tp")
+    step_out = r1 - len(carry_out)
+    even = even[(jnp.arange(extent) - step_out) % extent]
+    whole = wrap_ticks(even, 1)
     queries, new_keys, new_values = project_rows(whole, w_query, w_key, w_value)
     context = attend_all(queries, new_keys, new_values, k_cache, v_cache, cache_len)
     normed = finish_rows(context, arrived, w_out, ln_gain, ln_bias)

time: 178 us -> 165 us (0.927)
  waiting for transfers between devices: 64.4 us -> 42.6 us
  starting transfers between devices: 14.5 us -> 23.8 us
    all_gather x1 -> x0, waiting for transfers between devices: 22.3 us -> none  [shards(): whole = lax.all_gather(arrived, 'tp', axis=1, tiled=True)]
    ppermute x0 -> x3, starting transfers between devices: none -> 9.23 us  [the longest x2 6.79 us: shards(): jax.lax.ppermute(carry_out[-1] if carry_out else arrived, 'tp', arrivals)]
    ppermute x0 -> x3, waiting for transfers between devices: none -> 7.82 us  [the longest x2 7.82 us: shards(): jax.lax.ppermute(carry_out[-1] if carry_out else arrived, 'tp', arrivals)]
    reduce_scatter x1, waiting for transfers between devices: 27 us -> 19.7 us  [finish_rows(): lax.psum_scatter(partial_sum.astype(jnp.bfloat16), 'tp', scatter_dimensio...]
  transfers between devices with their start and end apart: 3 -> 5, of which waited for: 3 -> 4; matrix products, arithmetic and copies ran while one was open for 1% -> 1% of each run, Pallas kernels for 0% -> 0%
where the time goes in v1:
time: 165 us; the launch traced here: 164 us
  blocking collectives  43.3 us (26%)
  waiting for transfers between devices  42.6 us (26%)
  starting transfers between devices  23.8 us (14%)
  local copies, waits for them, and re-layouts  19 us (12%)
  matrix products  16.9 us (10%)
  between operations  13.6 us (8%)
  other arithmetic  4.95 us (3%)
    all_to_all x1, blocking collectives, shards(): lax.all_to_all(to_blocks(tokens)[send_order], 'req', split_axis=0, concat...  32.7 us
    reduce_scatter x1, waiting for transfers between devices, finish_rows(): lax.psum_scatter(partial_sum.astype(jnp.bfloat16), 'tp', scatter_dimensio...  19.7 us
    all_to_all x1, waiting for transfers between devices, shards(): lax.all_to_all(to_blocks(normed), 'req', split_axis=0, concat_axis=0, til...  15.1 us
    all_to_all x1, starting transfers between devices, shards(): lax.all_to_all(to_blocks(normed), 'req', split_axis=0, concat_axis=0, til...  14.6 us
    psum x1, blocking collectives, finish_rows(): lax.psum((jnp.sum(summed, axis=1), jnp.sum(summed * summed, axis=1)), 'tp')  10.6 us
    dynamic_slice x18, local copies, waits for them, and re-layouts, attend_all(): lax.map(lambda items: attend_padded(*items), (queries.reshape(req_shape),...  8.75 us
    ppermute x2, waiting for transfers between devices, shards(): jax.lax.ppermute(carry_out[-1] if carry_out else arrived, 'tp', arrivals)  7.82 us
    ppermute x2, starting transfers between devices, shards(): jax.lax.ppermute(carry_out[-1] if carry_out else arrived, 'tp', arrivals)  6.79 us
  transfers between devices with their start and end apart: 5, of which 4 were waited for; matrix products, arithmetic and copies ran while one was open for 1% of the time, Pallas kernels for 0%

profile of v1, /device:TPU:2, one launch (start us, length us, event | category | flops | bytes accessed | tf_op | source)
XLA Modules:
  0.0 164.3 jit_solution(2547496268408411676)
XLA Ops:
  6.5 0.7 compare_select_fusion.2
  7.3 1.0 scatter_custom_fusion
  8.3 1.0 reshape.195
  9.3 0.8 gather_fusion
  10.1 32.7 %all_to_all.10 = bf16[128,4,256]{2,1,0:T(4,128)(2,1)S(1)} all-to-all(bf16[128,4,256]{2,1,0:T(4,128)(2,1)S(1)} %gather_fusion), channel_id=1, replica_groups=mesh['req'=128,'tp'=4] {'req'}, dimensions={0} | all-to-all | bytes 524288 | tf_op jit(solution)/shard_map/all_to_all | solution.py:105
  42.9 3.4 %collective-permute-start = (bf16[512,256]{1,0:T(8,128)(2,1)S(1)}, bf16[512,256]{1,0:T(8,128)(2,1)S(1)}, u32[]{:S(2)}, u32[]{:S(2)}) collective-permute-start(bf16[512,256]{1,0:T(8,128)(2,1)S(1)} %reshape.196), channel_id=1, source_target_pairs={{0,1},{1,2},{2,3},{3,0},{4,5},{5,6},{6,7},{7,4},{8,9},{9,10},{10,1... | collective-permute-start | bytes 786440 | tf_op jit(solution)/shard_map/ppermute | solution.py:116
  46.3 2.4 %collective-permute-start.2 = (bf16[512,256]{1,0:T(8,128)(2,1)S(1)}, bf16[512,256]{1,0:T(8,128)(2,1)S(1)}, u32[]{:S(2)}, u32[]{:S(2)}) collective-permute-start(bf16[512,256]{1,0:T(8,128)(2,1)S(1)} %reshape.196), channel_id=1, source_target_pairs={{1,0},{2,1},{3,2},{0,3},{5,4},{6,5},{7,6},{4,7},{9,8},{10,9},{11,1... | collective-permute-start | bytes 786440 | tf_op jit(solution)/shard_map/ppermute | solution.py:119
  48.8 3.1 %collective-permute-done = bf16[512,256]{1,0:T(8,128)(2,1)S(1)} collective-permute-done((bf16[512,256]{1,0:T(8,128)(2,1)S(1)}, bf16[512,256]{1,0:T(8,128)(2,1)S(1)}, u32[]{:S(2)}, u32[]{:S(2)}) %collective-permute-start) | collective-permute-done | bytes 262176 | tf_op jit(solution)/shard_map/ppermute | solution.py:116
  51.9 3.4 %collective-permute-start.1 = (bf16[512,256]{1,0:T(8,128)(2,1)S(1)}, bf16[512,256]{1,0:T(8,128)(2,1)S(1)}, u32[]{:S(2)}, u32[]{:S(2)}) collective-permute-start(bf16[512,256]{1,0:T(8,128)(2,1)S(1)} %collective-permute-done), channel_id=1, source_target_pairs={{0,1},{1,2},{2,3},{3,0},{4,5},{5,6},{6,7},{7,4},{8,9},{9,10},{10,1... | collective-permute-start | bytes 786440 | tf_op jit(solution)/shard_map/ppermute | solution.py:116
  55.4 4.7 %collective-permute-done.1 = bf16[512,256]{1,0:T(8,128)(2,1)S(1)} collective-permute-done((bf16[512,256]{1,0:T(8,128)(2,1)S(1)}, bf16[512,256]{1,0:T(8,128)(2,1)S(1)}, u32[]{:S(2)}, u32[]{:S(2)}) %collective-permute-start.1) | collective-permute-done | bytes 262176 | tf_op jit(solution)/shard_map/ppermute | solution.py:116
  60.2 0.6 gather_fusion.1
  60.9 0.5 copy.17
  61.4 0.5 copy-done.8
  61.9 1.2 convolution_convert_fusion.3
  63.1 1.2 convolution_convert_fusion.2
  64.3 1.2 convolution_convert_fusion.1
  65.5 23.3 %while.12 = (s32[]{:T(128)}, bf16[2,256,256]{2,1,0:T(8,128)(2,1)}, bf16[2,1024,256]{2,1,0:T(8,128)(2,1)S(1)}, bf16[2,256,256]{2,1,0:T(8,128)(2,1)}, s32[2]{0:T(1...) while((s32[]{:T(128)}, bf16[2,256,256]{2,1,0:T(8,128)(2,1)}, ...), condition=%wide.region_4.5_spmd, body=%wide.region_1.4_spmd.sunk | while | flops 521149696 | bytes 12803309 | solution.py:48
  65.5 0.6 dynamic_slice.59
  66.2 0.6 iota_compare_fusion.4
  66.8 0.2 fusion.78
  67.0 1.1 constant_dynamic-slice_fusion.9
  68.4 1.0 constant_dynamic-slice_fusion.10
  69.6 2.3 %fusion.79 = f32[4,256]{1,0:T(4,128)S(1)} fusion(pred[256,1280]{1,0:T(8,128)(4,1)S(1)} %fusion.78, bf16[256,4,64]{0,2,1:T(8,128)(2,1)S(1)} %bitcast.61, bf16[256,4,64]{0,2,1:T(8,128)(2,1)S(1)} %bitcast.63, bf16[1024,4,64]{0,2,1:T(8,128)(2,1)S(1)} %bitcast.57), kind=kOutput, calls=%fused_computation.8.clone.1 | convolution fusion | flops 175637760 | bytes 1118208 | tf_op jit(solution)/shard_map/while/body/eval_jaxpr/sub | solution.py:36
  71.9 0.2 copy.38
  72.2 0.9 constant_dynamic-slice_fusion.8
  73.2 3.1 %fusion.80 = bf16[256,4,64]{0,2,1:T(8,128)(2,1)S(1)} fusion(pred[256,1280]{1,0:T(8,128)(4,1)S(1)} %fusion.78, bf16[256,4,64]{0,2,1:T(8,128)(2,1)S(1)} %bitcast.65, bf16[1024,4,64]{0,2,1:T(8,128)(2,1)S(1)} %bitcast.59, bf16[256,4,64]{0,2,1:T(8,128)(2,1)} %bitcast.62, bf16[256,4,64]{0,2,1:T(8,128)(2,1)} %bitcast.64, ...), kind=kOutput, calls=%fused_computation.17.clone.1 | convolution fusion | flops 344852736 | bytes 1904640 | tf_op jit(solution)/shard_map/while/body/eval_jaxpr/hqk,khd->qhd/dot_general | solution.py:38
  76.5 0.7 copy-done.7
  77.2 0.6 dynamic_slice.59
  77.8 0.6 iota_compare_fusion.4
  78.5 0.2 fusion.78
  78.7 1.1 constant_dynamic-slice_fusion.9
  80.0 1.0 constant_dynamic-slice_fusion.10
  81.2 2.3 %fusion.79 = f32[4,256]{1,0:T(4,128)S(1)} fusion(pred[256,1280]{1,0:T(8,128)(4,1)S(1)} %fusion.78, bf16[256,4,64]{0,2,1:T(8,128)(2,1)S(1)} %bitcast.61, bf16[256,4,64]{0,2,1:T(8,128)(2,1)S(1)} %bitcast.63, bf16[1024,4,64]{0,2,1:T(8,128)(2,1)S(1)} %bitcast.57), kind=kOutput, calls=%fused_computation.8.clone.1 | convolution fusion | flops 175637760 | bytes 1118208 | tf_op jit(solution)/shard_map/while/body/eval_jaxpr/sub | solution.py:36
  83.8 0.9 constant_dynamic-slice_fusion.8
  84.8 3.1 %fusion.80 = bf16[256,4,64]{0,2,1:T(8,128)(2,1)S(1)} fusion(pred[256,1280]{1,0:T(8,128)(4,1)S(1)} %fusion.78, bf16[256,4,64]{0,2,1:T(8,128)(2,1)S(1)} %bitcast.65, bf16[1024,4,64]{0,2,1:T(8,128)(2,1)S(1)} %bitcast.59, bf16[256,4,64]{0,2,1:T(8,128)(2,1)} %bitcast.62, bf16[256,4,64]{0,2,1:T(8,128)(2,1)} %bitcast.64, ...), kind=kOutput, calls=%fused_computation.17.clone.1 | convolution fusion | flops 344852736 | bytes 1904640 | tf_op jit(solution)/shard_map/while/body/eval_jaxpr/hqk,khd->qhd/dot_general | solution.py:38
  88.1 0.7 copy-done.7
  88.8 2.4 %convolution_convert_fusion = bf16[512,1024]{1,0:T(8,128)(2,1)} fusion(bf16[512,256]{1,0:T(8,128)(2,1)} %bitcast.73, bf16[256,1024]{1,0:T(8,128)(2,1)S(1)} %copy-done), kind=kOutput, calls=%fused_computation.42 | convolution fusion | flops 268959744 | bytes 1835008 | tf_op jit(solution)/shard_map/dot_general | solution.py:71
  91.3 0.8 dynamic_slice.45
  92.0 0.8 dynamic_slice.46
  92.8 19.7 %reduce-scatter.2.cloned.1.call-done = bf16[512,256]{1,0:T(8,128)(2,1)} async-done(((bf16[512,1024]{1,0:T(8,128)(2,1)}), bf16[512,256]{1,0:T(8,128)(2,1)}) %reduce-scatter.2.cloned.1.call-update) | async-done | bytes 262160 | tf_op jit(solution)/shard_map/reduce_scatter | solution.py:72
  112.5 1.2 fusion.46
  113.6 10.6 %all-reduce = (f32[512]{0:T(512)S(1)}, f32[512]{0:T(512)S(1)}) all-reduce(f32[512]{0:T(512)S(1)} %get-tuple-element.124, f32[512]{0:T(512)S(1)} %get-tuple-element.123), channel_id=1, replica_groups=mesh['req'=128,'tp'=4] {'tp'}, use_global_device_ids=true, to_apply=%region_9.10 | all-reduce | flops 1024 | bytes 8192 | tf_op jit(solution)/shard_map/psum | solution.py:76
  124.2 1.2 add_convert_fusion
  125.4 0.8 reshape.202
  126.2 14.6 %all-to-all-start.1 = ((bf16[128,4,256]{2,1,0:T(4,128)(2,1)}), bf16[128,4,256]{2,1,0:T(4,128)(2,1)S(1)}, u32[]{:S(2)}, u32[]{:S(2)}) async-start(bf16[128,4,256]{2,1,0:T(4,128)(2,1)} %reshape.202), calls=%async_computation.2 | async-start | bytes 524288 | tf_op jit(solution)/shard_map/all_to_all | solution.py:130
  140.7 15.1 %all-to-all-done.1 = bf16[128,4,256]{2,1,0:T(4,128)(2,1)S(1)} async-done(((bf16[128,4,256]{2,1,0:T(4,128)(2,1)}), bf16[128,4,256]{2,1,0:T(4,128)(2,1)S(1)}, u32[]{:S(2)}, u32[]{:S(2)}) %all-to-all-start.1) | async-done | bytes 262176 | tf_op jit(solution)/shard_map/all_to_all | solution.py:130
  155.8 0.8 gather_fusion.2
  156.6 0.8 reshape.203
  (58 shorter events, 1.9 us)
Async XLA Ops:
  6.5 82.3 %copy-start = (bf16[256,1024]{1,0:T(8,128)(2,1)S(1)}, bf16[256,1024]{1,0:T(8,128)(2,1)}, u32[]{:S(2)}) copy-start(bf16[256,1024]{1,0:T(8,128)(2,1)} %param.19) | copy-start | bytes 1572868
  6.5 105.9 %reduce-scatter.2.cloned.1.call-start = ((), (), s32[]{:S(2)}) async-start(), calls=%async_computation.3 | async-start | bytes 1310720 | tf_op jit(solution)/shard_map/reduce_scatter | solution.py:72
  42.9 17.2 %copy-start.4 = (bf16[512,256]{1,0:T(8,128)(2,1)}, bf16[512,256]{1,0:T(8,128)(2,1)S(1)}, u32[]{:S(2)}) copy-start(bf16[512,256]{1,0:T(8,128)(2,1)S(1)} %reshape.196) | copy-start | bytes 786436
  42.9 8.9 %collective-permute-start = (bf16[512,256]{1,0:T(8,128)(2,1)S(1)}, bf16[512,256]{1,0:T(8,128)(2,1)S(1)}, u32[]{:S(2)}, u32[]{:S(2)}) collective-permute-start(bf16[512,256]{1,0:T(8,128)(2,1)S(1)} %reshape.196), channel_id=1, source_target_pairs={{0,1},{1,2},{2,3},{3,0},{4,5},{5,6},{6,7},{7,4},{8,9},{9,10},{10,1... | collective-permute-start | bytes 786440 | tf_op jit(solution)/shard_map/ppermute | solution.py:116
  46.3 9.1 %collective-permute-start.2 = (bf16[512,256]{1,0:T(8,128)(2,1)S(1)}, bf16[512,256]{1,0:T(8,128)(2,1)S(1)}, u32[]{:S(2)}, u32[]{:S(2)}) collective-permute-start(bf16[512,256]{1,0:T(8,128)(2,1)S(1)} %reshape.196), channel_id=1, source_target_pairs={{1,0},{2,1},{3,2},{0,3},{5,4},{6,5},{7,6},{4,7},{9,8},{10,9},{11,1... | collective-permute-start | bytes 786440 | tf_op jit(solution)/shard_map/ppermute | solution.py:119
  51.9 8.3 %collective-permute-start.1 = (bf16[512,256]{1,0:T(8,128)(2,1)S(1)}, bf16[512,256]{1,0:T(8,128)(2,1)S(1)}, u32[]{:S(2)}, u32[]{:S(2)}) collective-permute-start(bf16[512,256]{1,0:T(8,128)(2,1)S(1)} %collective-permute-done), channel_id=1, source_target_pairs={{0,1},{1,2},{2,3},{3,0},{4,5},{5,6},{6,7},{7,4},{8,9},{9,10},{10,1... | collective-permute-start | bytes 786440 | tf_op jit(solution)/shard_map/ppermute | solution.py:116
  60.9 1.0 copy-start.8
  61.9 1.2 copy-start.9
  63.1 1.2 copy-start.10
  64.3 1.2 copy-start.1
  64.3 1.2 copy-start.11
  69.5 2.5 %copy-start.2 = (bf16[1,256,256]{1,2,0:T(8,128)(2,1)}, bf16[1,256,256]{1,2,0:T(8,128)(2,1)S(1)}, u32[]{:S(2)}) copy-start(bf16[1,256,256]{1,2,0:T(8,128)(2,1)S(1)} %copy.39) | copy-start | bytes 393220 | tf_op jit(solution)/shard_map/while
  69.6 2.3 %copy-start.3 = (bf16[1,256,256]{1,2,0:T(8,128)(2,1)}, bf16[1,256,256]{1,2,0:T(8,128)(2,1)S(1)}, u32[]{:S(2)}) copy-start(bf16[1,256,256]{1,2,0:T(8,128)(2,1)S(1)} %copy.40) | copy-start | bytes 393220 | tf_op jit(solution)/shard_map/while
  73.2 3.3 %copy-start.6 = (bf16[2,256,256]{2,1,0:T(8,128)(2,1)S(1)}, bf16[2,256,256]{2,1,0:T(8,128)(2,1)}, u32[]{:S(2)}) copy-start(bf16[2,256,256]{2,1,0:T(8,128)(2,1)} %get-tuple-element.222) | copy-start | bytes 786436 | tf_op jit(solution)/shard_map/while
  76.5 0.7 copy-start.7
  81.1 2.5 %copy-start.2 = (bf16[1,256,256]{1,2,0:T(8,128)(2,1)}, bf16[1,256,256]{1,2,0:T(8,128)(2,1)S(1)}, u32[]{:S(2)}) copy-start(bf16[1,256,256]{1,2,0:T(8,128)(2,1)S(1)} %copy.39) | copy-start | bytes 393220 | tf_op jit(solution)/shard_map/while
  81.2 2.3 %copy-start.3 = (bf16[1,256,256]{1,2,0:T(8,128)(2,1)}, bf16[1,256,256]{1,2,0:T(8,128)(2,1)S(1)}, u32[]{:S(2)}) copy-start(bf16[1,256,256]{1,2,0:T(8,128)(2,1)S(1)} %copy.40) | copy-start | bytes 393220 | tf_op jit(solution)/shard_map/while
  84.8 3.3 %copy-start.6 = (bf16[2,256,256]{2,1,0:T(8,128)(2,1)S(1)}, bf16[2,256,256]{2,1,0:T(8,128)(2,1)}, u32[]{:S(2)}) copy-start(bf16[2,256,256]{2,1,0:T(8,128)(2,1)} %get-tuple-element.222) | copy-start | bytes 786436 | tf_op jit(solution)/shard_map/while
  88.1 0.7 copy-start.7
  88.8 23.6 %copy-start.5 = (bf16[512,256]{1,0:T(8,128)(2,1)S(1)}, bf16[512,256]{1,0:T(8,128)(2,1)}, u32[]{:S(2)}) copy-start(bf16[512,256]{1,0:T(8,128)(2,1)} %copy-done.4) | copy-start | bytes 786436
  126.2 29.7 %all-to-all-start.1 = ((bf16[128,4,256]{2,1,0:T(4,128)(2,1)}), bf16[128,4,256]{2,1,0:T(4,128)(2,1)S(1)}, u32[]{:S(2)}, u32[]{:S(2)}) async-start(bf16[128,4,256]{2,1,0:T(4,128)(2,1)} %reshape.202), calls=%async_computation.2 | async-start | bytes 524288 | tf_op jit(solution)/shard_map/all_to_all | solution.py:130
Sparse Core Ops, SparseCore 0:
  91.4 21.0 reduce-scatter.1
